TPU v7x, 256 devices: a whole 4x4x8 slice. The times are simulated.
256 devices in a mesh: pair: 2 (over core), seq: 32 (over y, x, z_hi), tp: 4 (over z_lo).
Axes of the slice: x: 4, y: 4, z: 8 (z_hi: 2, z_lo: 4; z = z_hi * 4 + z_lo), core: 2. Of those that a mesh axis runs over, the one named last changes fastest.
Arguments:
- hidden: bfloat16 [36864, 3072], P(('pair', 'seq'), 'tp'), may hold values from -11 to 11
- positions: int32 [3, 36864], P(None, ('pair', 'seq')), may hold values from 0 to 63, as said below
- lengths: int32 [8], P('pair'), may hold values from 1 to 512, as said below
- step_index: int32 [1], replicated, may hold values from 0 to 7
- layer_mod: float32 [8, 3, 3072], P('pair'), may hold values from -3 to 3
- final_mod: float32 [8, 2, 3072], P('pair'), may hold values from -3 to 3
- qkv_weight: bfloat16 [3072, 3, 1536], P(None, None, 'tp'), may hold values from -0.108253175 to 0.108253175
- q_gain: float32 [128], replicated, may hold values from 0.5 to 5.5
- k_gain: float32 [128], replicated, may hold values from 0.5 to 5.5
- out_weight: bfloat16 [1536, 3072], P('tp'), may hold values from -0.15625 to 0.15625
- final_weight: bfloat16 [3072, 64], P('tp'), may hold values from -0.109375 to 0.109375
- latents: float32 [16384, 64], P(('pair', 'seq')), may hold values from -6 to 6
Outputs:
- new_hidden: bfloat16 [36864, 3072], P(('pair', 'seq'), 'tp')
- attention_lse: float32 [12, 36864], P('tp', ('pair', 'seq'))
- next_latents: float32 [16384, 64], P(('pair', 'seq'))
Inputs may be any that keep to these rules, and one draw needn't show every extreme that they name: `lengths`: some sequence has all 512 text tokens live and some sequence just one. `positions`: the first component is zero; text rows are zero; the image rows of a sequence hold each cell (row, column) of a grid 64 cells wide exactly once, the same for both sequences of a prompt.
All inputs are finite; a program needn't handle non-finite values.
Results may differ from a plain program's by a relative error of at most 0.01.
Values may be sent and summed in bfloat16 or wider, within the bound.
No kernel may reach another device: no remote copies, remote signals or barrier semaphores. Data moves between devices by JAX's collectives and lax.ppermute only.
A program may use at most 128 MiB of HBM per device.

v0:
```python
import jax
import jax.numpy as jnp
from jax import lax
from jax.sharding import PartitionSpec as P

ROPE_T = 16
ROPE_H = 56
ROPE_W = 56
STEPS = 8
IMG_DEV = 512
TXT_DEV = 64
GUIDE = 3.5
SHIFT = 3.0


def swapped(block, axis, bit):
    count = lax.axis_size(axis)
    route = []
    for low in range(count):
        high = low | 1 << bit
        if high != low and high < count:
            route += [(low, high), (high, low)]
    return lax.ppermute(block, axis, route)


def rope_angles(ids_block):
    angle_parts = []
    for axis_pos, rope_width in ((0, ROPE_T), (1, ROPE_H), (2, ROPE_W)):
        frequencies = 10000.0 ** (-jnp.arange(0, rope_width, 2).astype(jnp.float32) / rope_width)
        angle_parts.append(ids_block[axis_pos].astype(jnp.float32)[:, None] * frequencies[None, :])
    angles = jnp.concatenate(angle_parts, axis=1)
    return (jnp.cos(angles), jnp.sin(angles))


def rotate(tensor, cosine, sine_part):
    dims_in = tensor.shape
    pair_view = tensor.reshape(dims_in[0], dims_in[1], dims_in[2] // 2, 2)
    first_part = pair_view[..., 0]
    second_part = pair_view[..., 1]
    cosine = cosine[:, None, :]
    sine_part = sine_part[:, None, :]
    turned = jnp.stack(
        [
            cosine * first_part - sine_part * second_part,
            sine_part * first_part + cosine * second_part,
        ],
        axis=-1,
    )
    return turned.reshape(dims_in)


def rms_gain(tensor, gain_vec):
    return tensor * lax.rsqrt(jnp.mean(tensor * tensor, axis=-1, keepdims=True) + 1e-06) * gain_vec


def modulate(features, shift_vec, scale_vec):
    row_mean = jnp.mean(features, axis=-1, keepdims=True)
    row_var = jnp.mean(features * features, axis=-1, keepdims=True) - row_mean * row_mean
    return (features - row_mean) * lax.rsqrt(row_var + 1e-06) * (1.0 + scale_vec) + shift_vec


def sigma_at(step_now):
    time_now = 1.0 - step_now.astype(jnp.float32) / STEPS
    return SHIFT * time_now / (1.0 + (SHIFT - 1.0) * time_now)


def attend_block(softmax_state, queries, packet, anchor, text_count):
    rows_dev = IMG_DEV + TXT_DEV
    piece_count = packet.shape[1] // rows_dev
    offset = jnp.arange(rows_dev, dtype=jnp.int32)
    score_scale = queries.shape[-1] ** (-0.5)

    def fold_piece(piece_idx, carried):
        row_max, row_sum, weighted = carried
        key_piece = lax.dynamic_slice_in_dim(packet, piece_idx * rows_dev, rows_dev, 1)
        text_index = (anchor + piece_idx) * TXT_DEV + offset - IMG_DEV
        is_live = (offset < IMG_DEV) | (text_index < text_count)
        scores = (
            jnp.einsum("qhd,khd->hqk", queries, key_piece[0], preferred_element_type=jnp.float32)
            * score_scale
        )
        scores = jnp.where(is_live[None, None, :], scores, -jnp.inf)
        new_max = jnp.maximum(row_max, jnp.max(scores, axis=2))
        exps = jnp.exp(scores - new_max[:, :, None])
        decay = jnp.exp(row_max - new_max)
        row_sum = row_sum * decay + jnp.sum(exps, axis=2)
        weighted = weighted * decay[:, :, None] + jnp.einsum(
            "hqk,khd->hqd",
            exps.astype(jnp.bfloat16),
            key_piece[1],
            preferred_element_type=jnp.float32,
        )
        return (new_max, row_sum, weighted)

    return lax.fori_loop(0, piece_count, fold_piece, softmax_state)


def on_device(
    hidden,
    positions,
    lengths,
    step_index,
    layer_mod,
    final_mod,
    qkv_weight,
    q_gain,
    k_gain,
    out_weight,
    final_weight,
    latents,
):
    spread = lax.axis_size("seq") // 4
    bit_count = spread.bit_length() - 1
    seq_pos = lax.axis_index("seq")
    local_seq = seq_pos // spread
    shard_pos = seq_pos % spread
    tp_pos = lax.axis_index("tp")
    local_width = hidden.shape[1]
    gathered = lax.all_gather(hidden, "tp", axis=1, tiled=True)
    model_width = gathered.shape[1]
    rows_dev = gathered.shape[0]
    layer_terms = lax.dynamic_index_in_dim(layer_mod, local_seq, 0, keepdims=False)
    text_count = lax.dynamic_index_in_dim(lengths, local_seq, 0, keepdims=False)
    modulated = modulate(gathered.astype(jnp.float32), layer_terms[0], layer_terms[1]).astype(
        jnp.bfloat16
    )
    head_dim = q_gain.shape[0]
    head_cols = qkv_weight.shape[2]
    heads_here = head_cols // head_dim
    projected = jnp.dot(
        modulated,
        qkv_weight.reshape(model_width, 3 * head_cols),
        preferred_element_type=jnp.float32,
    )
    projected = projected.reshape(rows_dev, 3, heads_here, head_dim)
    cosine, sine_part = rope_angles(positions)
    queries = rotate(rms_gain(projected[:, 0], q_gain), cosine, sine_part).astype(jnp.bfloat16)
    key_rot = rotate(rms_gain(projected[:, 1], k_gain), cosine, sine_part).astype(jnp.bfloat16)
    values = projected[:, 2].astype(jnp.bfloat16)
    packet = jnp.stack([key_rot, values])
    softmax_state = (
        jnp.full((heads_here, rows_dev), -jnp.inf, jnp.float32),
        jnp.zeros((heads_here, rows_dev), jnp.float32),
        jnp.zeros((heads_here, rows_dev, head_dim), jnp.float32),
    )
    held_keys = packet
    for bit_pos in range(bit_count):
        far_keys = swapped(held_keys, "seq", bit_pos)
        block_size = 1 << bit_pos
        lower_half = shard_pos // block_size % 2 == 0
        held_keys = jnp.where(
            lower_half,
            jnp.concatenate([held_keys, far_keys], axis=1),
            jnp.concatenate([far_keys, held_keys], axis=1),
        )
    softmax_state = attend_block(softmax_state, queries, held_keys, 0, text_count)
    row_max, row_sum, weighted = softmax_state
    attended = (weighted / row_sum[:, :, None]).astype(jnp.bfloat16)
    log_sums = row_max + jnp.log(row_sum)
    attn_flat = attended.transpose(1, 0, 2).reshape(rows_dev, head_cols)
    partial_out = jnp.dot(attn_flat, out_weight, preferred_element_type=jnp.float32)
    update = lax.psum_scatter(
        partial_out.astype(jnp.bfloat16), "tp", scatter_dimension=1, tiled=True
    ).astype(jnp.float32)
    gate_slice = lax.dynamic_slice_in_dim(layer_terms[2], tp_pos * local_width, local_width, 0)
    new_hidden = (hidden.astype(jnp.float32) + gate_slice * update).astype(jnp.bfloat16)
    final_terms = lax.dynamic_index_in_dim(final_mod, local_seq, 0, keepdims=False)
    final_shift = lax.dynamic_slice_in_dim(final_terms[0], tp_pos * local_width, local_width, 0)
    final_scale = lax.dynamic_slice_in_dim(final_terms[1], tp_pos * local_width, local_width, 0)
    image_rows = new_hidden[:IMG_DEV].astype(jnp.float32)
    weight = final_weight.astype(jnp.float32)
    row_sums = jnp.sum(image_rows, axis=1)
    squares = jnp.sum(image_rows * image_rows, axis=1)
    row_sums, squares = lax.psum((row_sums, squares), "tp")
    row_mean = row_sums / model_width
    inv_std = lax.rsqrt(squares / model_width - row_mean * row_mean + 1e-06)
    final_in = (image_rows - row_mean[:, None]) * inv_std[:, None] * (
        1.0 + final_scale
    ) + final_shift
    velocity = lax.psum(
        jnp.dot(final_in, weight, precision=lax.Precision.HIGHEST).astype(jnp.bfloat16), "tp"
    ).astype(jnp.float32)
    half_rows = IMG_DEV // 2
    is_cond = local_seq % 2 == 0
    outgoing = jnp.where(is_cond, velocity[half_rows:], velocity[:half_rows])
    partner_half = swapped(outgoing.astype(jnp.bfloat16), "seq", bit_count).astype(outgoing.dtype)
    own_half = jnp.where(is_cond, velocity[:half_rows], velocity[half_rows:])
    cond_vel = jnp.where(is_cond, own_half, partner_half)
    uncond_vel = jnp.where(is_cond, partner_half, own_half)
    guided = uncond_vel + GUIDE * (cond_vel - uncond_vel)
    step_now = step_index[0]
    time_step = sigma_at(step_now + 1) - sigma_at(step_now)
    return (new_hidden, log_sums, latents + time_step * guided)


def solution(mesh):
    return jax.shard_map(
        on_device,
        mesh=mesh,
        in_specs=(
            P(("pair", "seq"), "tp"),
            P(None, ("pair", "seq")),
            P("pair"),
            P(),
            P("pair", None, None),
            P("pair", None, None),
            P(None, None, "tp"),
            P(),
            P(),
            P("tp", None),
            P("tp", None),
            P(("pair", "seq"), None),
        ),
        out_specs=(P(("pair", "seq"), "tp"), P("tp", ("pair", "seq")), P(("pair", "seq"), None)),
        check_vma=False,
    )
```

profile of v0, /device:TPU:2, one launch (start us, length us, event | category | flops | bytes accessed | tf_op | source)
XLA Modules:
  0.0 560.9 jit_solution(13021237416934958148)
XLA Ops:
  8.0 10.3 %copy.17 = bf16[3072,3,384]{0,2,1:T(8,128)(2,1)} copy(bf16[3072,3,384]{2,0,1:T(8,128)(2,1)} %param.20) | data formatting | bytes 14155776 | tf_op args[6]
  20.3 65.6 %all-gather.2.cloned.1.call-done = bf16[576,3072]{1,0:T(8,128)(2,1)} async-done(((bf16[576,768]{1,0:T(8,128)(2,1)}), bf16[576,3072]{1,0:T(8,128)(2,1)}) %all-gather.2.cloned.1.call-update) | async-done | bytes 3538960 | tf_op jit(solution)/shard_map/all_gather | solution.py:119
  89.2 8.0 %fusion.26 = f32[576,3,3,128]{3,0,2,1:T(8,128)S(1)} fusion(bf16[3,3,128,3072]{3,2,1,0:T(8,128)(2,1)} %bitcast.68, bf16[576,3072]{1,0:T(8,128)(2,1)S(1)} %copy-done.1, f32[3072]{0:T(1024)S(1)} %bitcast.71, f32[3072]{0:T(1024)S(1)} %bitcast.70, f32[576]{0:T(1024)S(1)} %get-tuple-element.306, f32[576]{0:T(1024)S(1)} %get-tuple-element.305), kind=kOutput, calls=%fused_computation.38 | convolution fusion | flops 4087480320 | bytes 13300224 | tf_op jit(solution)/shard_map/dot_general | solution.py:130
  122.5 4.5 collective-permute-start
  127.0 30.3 %collective-permute-done = bf16[2,576,3,128]{3,1,2,0:T(8,128)(2,1)} collective-permute-done((bf16[2,576,3,128]{3,1,2,0:T(8,128)(2,1)}, bf16[2,576,3,128]{3,1,2,0:T(8,128)(2,1)}, u32[]{:S(2)}, u32[]{:S(2)}) %collective-permute-start) | collective-permute-done | bytes 884768 | tf_op jit(solution)/shard_map/ppermute | solution.py:23
  161.0 39.1 %collective-permute-done.1 = bf16[2,1152,3,128]{3,1,2,0:T(8,128)(2,1)} collective-permute-done((bf16[2,1152,3,128]{3,1,2,0:T(8,128)(2,1)}, bf16[2,1152,3,128]{3,1,2,0:T(8,128)(2,1)}, u32[]{:S(2)}, u32[]{:S(2)}) %collective-permute-start.1) | collective-permute-done | bytes 1769504 | tf_op jit(solution)/shard_map/ppermute | solution.py:23
  200.1 5.3 maximum_select_fusion.1
  211.6 71.9 %collective-permute-done.2 = bf16[2,2304,3,128]{3,1,2,0:T(8,128)(2,1)} collective-permute-done((bf16[2,2304,3,128]{3,1,2,0:T(8,128)(2,1)}, bf16[2,2304,3,128]{3,1,2,0:T(8,128)(2,1)}, u32[]{:S(2)}, u32[]{:S(2)}) %collective-permute-start.2) | collective-permute-done | bytes 3538976 | tf_op jit(solution)/shard_map/ppermute | solution.py:23
  283.5 9.3 %maximum_select_fusion = bf16[2,4608,3,128]{3,1,2,0:T(8,128)(2,1)} fusion(bf16[2,2304,3,128]{3,1,2,0:T(8,128)(2,1)} %collective-permute-done.2, bf16[2,2304,3,128]{3,1,2,0:T(8,128)(2,1)} %maximum_select_fusion.1, pred[]{:T(512)S(6)} %eq.18), kind=kLoop, calls=%fused_computation.35 | loop fusion | flops 31850496 | bytes 14155777 | tf_op jit(solution)/shard_map/jit(_where)/select_n | solution.py:151
  292.8 102.5 %while.21 = (s32[]{:T(128)}, f32[3,576]{1,0:T(4,128)S(1)}, f32[3,576]{1,0:T(4,128)S(1)}, f32[3,576,128]{2,1,0:T(8,128)}, s32[]{:T(128)}, /*index=5*/bf16[2,4608,...) while((s32[]{:T(128)}, f32[3,576]{1,0:T(4,128)S(1)}, ...), condition=%wide.region_7.8_spmd.clone.clone, body=%wide.region_4.7_spmd.clone.clone.sunk | while | flops 521231616 | bytes 15596003 | solution.py:95
  300.7 4.7 fusion.72
  313.3 5.0 fusion.72
  326.1 5.0 fusion.72
  331.7 3.9 bitcast_reduce_fusion.2
  339.0 5.0 fusion.72
  344.6 3.9 bitcast_reduce_fusion.2
  351.8 5.0 fusion.72
  364.7 5.0 fusion.72
  370.3 3.9 bitcast_reduce_fusion.2
  377.5 5.0 fusion.72
  390.3 5.0 fusion.72
  402.7 80.0 %reduce-scatter.2.cloned.1.call-done = bf16[576,768]{1,0:T(8,128)(2,1)} async-done(((bf16[576,3072]{1,0:T(8,128)(2,1)}), bf16[576,768]{1,0:T(8,128)(2,1)}) %reduce-scatter.2.cloned.1.call-update) | async-done | bytes 884752 | tf_op jit(solution)/shard_map/reduce_scatter | solution.py:162
  485.4 10.7 %all-reduce = (f32[512]{0:T(512)S(1)}, f32[512]{0:T(512)S(1)}) all-reduce(f32[512]{0:T(512)S(1)} %get-tuple-element.267, f32[512]{0:T(512)S(1)} %get-tuple-element.266), channel_id=1, replica_groups=mesh['pair'=2,'seq'=32,'tp'=4] {'tp'}, use_global_device_ids=true, to_apply=%region_12.13 | all-reduce | flops 1024 | bytes 8192 | tf_op jit(solution)/shard_map/psum | solution.py:174
  499.9 48.9 %all-reduce.3.cloned.1.call-done = bf16[512,64]{0,1:T(8,128)(2,1)} async-done(((bf16[512,64]{0,1:T(8,128)(2,1)}), bf16[512,64]{0,1:T(8,128)(2,1)}) %all-reduce.3.cloned.1.call-update) | async-done | bytes 65552 | tf_op jit(solution)/shard_map/psum | solution.py:180
  (125 shorter events, 110.8 us)
Async XLA Ops:
  7.2 389.9 %copy-start = (bf16[384,3072]{1,0:T(8,128)(2,1)S(1)}, bf16[384,3072]{1,0:T(8,128)(2,1)}, u32[]{:S(2)}) copy-start(bf16[384,3072]{1,0:T(8,128)(2,1)} %param.23) | copy-start | bytes 7077892
  7.2 78.7 %all-gather.2.cloned.1.call-start = ((), (), s32[]{:S(2)}) async-start(), calls=%async_computation.1 | async-start | bytes 4423680 | tf_op jit(solution)/shard_map/all_gather | solution.py:119
  7.9 474.8 %reduce-scatter.2.cloned.1.call-start = ((), (), s32[]{:S(2)}) async-start(), calls=%async_computation.2 | async-start | bytes 4423680 | tf_op jit(solution)/shard_map/reduce_scatter | solution.py:162
  8.0 10.3 %copy-start.8 = (f32[128]{0:T(128)S(1)}, f32[128]{0:T(128)}, u32[]{:S(2)}) copy-start(f32[128]{0:T(128)} %param.22) | copy-start | bytes 1540
  8.0 10.4 %copy-start.9 = (f32[128]{0:T(128)S(1)}, f32[128]{0:T(128)}, u32[]{:S(2)}) copy-start(f32[128]{0:T(128)} %param.21) | copy-start | bytes 1540
  8.0 10.6 %copy-start.7 = (s32[3,576]{1,0:T(4,128)S(1)}, s32[3,576]{1,0:T(4,128)}, u32[]{:S(2)}) copy-start(s32[3,576]{1,0:T(4,128)} %param.15) | copy-start | bytes 20740
  85.9 3.3 copy-start.1
  122.5 34.9 %collective-permute-start = (bf16[2,576,3,128]{3,1,2,0:T(8,128)(2,1)}, bf16[2,576,3,128]{3,1,2,0:T(8,128)(2,1)}, u32[]{:S(2)}, u32[]{:S(2)}) collective-permute-start(bf16[2,576,3,128]{3,1,2,0:T(8,128)(2,1)} %pad_maximum_fusion), channel_id=1, source_target_pairs={{0,4},{4,0},{8,12},{12,8},{16,20},{20,16},{24,28},{28,24},{32,36},... | collective-permute-start | bytes 2654216 | tf_op jit(solution)/shard_map/ppermute | solution.py:23
  160.4 39.7 %collective-permute-start.1 = (bf16[2,1152,3,128]{3,1,2,0:T(8,128)(2,1)}, bf16[2,1152,3,128]{3,1,2,0:T(8,128)(2,1)}, u32[]{:S(2)}, u32[]{:S(2)}) collective-permute-start(bf16[2,1152,3,128]{3,1,2,0:T(8,128)(2,1)} %maximum_select_fusion.2), channel_id=1, source_target_pairs={{0,8},{8,0},{4,12},{12,4},{16,24},{24,16},{20,28},{28,20},{32,40},... | collective-permute-start | bytes 5308424 | tf_op jit(solution)/shard_map/ppermute | solution.py:23
  161.0 46.4 %copy-start.11 = (s32[4]{0:T(128)S(1)}, s32[4]{0:T(128)}, u32[]{:S(2)}) copy-start(s32[4]{0:T(128)} %param.16) | copy-start | bytes 52
  161.0 47.0 %copy-start.4 = (bf16[576,3,64,1]{0,3,2,1:T(2,128)(2,1)S(1)}, bf16[576,3,64,1]{0,3,2,1:T(2,128)(2,1)}, u32[]{:S(2)}) copy-start(bf16[576,3,64,1]{0,3,2,1:T(2,128)(2,1)} %get-tuple-element.295) | copy-start | bytes 663556
  161.0 47.0 %copy-start.5 = (bf16[576,3,64,1]{0,3,2,1:T(2,128)(2,1)S(1)}, bf16[576,3,64,1]{0,3,2,1:T(2,128)(2,1)}, u32[]{:S(2)}) copy-start(bf16[576,3,64,1]{0,3,2,1:T(2,128)(2,1)} %get-tuple-element.296) | copy-start | bytes 663556
  205.4 78.2 %collective-permute-start.2 = (bf16[2,2304,3,128]{3,1,2,0:T(8,128)(2,1)}, bf16[2,2304,3,128]{3,1,2,0:T(8,128)(2,1)}, u32[]{:S(2)}, u32[]{:S(2)}) collective-permute-start(bf16[2,2304,3,128]{3,1,2,0:T(8,128)(2,1)} %maximum_select_fusion.1), channel_id=1, source_target_pairs={{0,16},{16,0},{4,20},{20,4},{8,24},{24,8},{12,28},{28,12},{32,48},... | collective-permute-start | bytes 10616840 | tf_op jit(solution)/shard_map/ppermute | solution.py:23
  400.8 81.8 %copy-start.2 = (bf16[576,768]{1,0:T(8,128)(2,1)S(1)}, bf16[576,768]{1,0:T(8,128)(2,1)}, u32[]{:S(2)}) copy-start(bf16[576,768]{1,0:T(8,128)(2,1)} %param.14) | copy-start | bytes 2654212
  400.8 95.3 %copy-start.10 = (bf16[768,64]{0,1:T(8,128)(2,1)S(1)}, bf16[768,64]{0,1:T(8,128)(2,1)}, u32[]{:S(2)}) copy-start(bf16[768,64]{0,1:T(8,128)(2,1)} %param.24) | copy-start | bytes 294916
  400.9 152.8 %copy-start.6 = (f32[256,64]{0,1:T(8,128)S(1)}, f32[256,64]{0,1:T(8,128)}, u32[]{:S(2)}) copy-start(f32[256,64]{0,1:T(8,128)} %param.25) | copy-start | bytes 196612
  400.9 147.9 %all-reduce.3.cloned.1.call-start = ((), (), s32[]{:S(2)}) async-start(), calls=%async_computation.3 | async-start | bytes 131072 | tf_op jit(solution)/shard_map/psum | solution.py:180
  484.1 0.9 copy-start.3
  549.7 4.0 collective-permute-start.3
Sparse Core Ops, SparseCore 0:
  9.8 76.0 all-gather.1
  401.0 81.6 reduce-scatter.1
  499.3 49.4 all-reduce.2
where the time goes:
time: 563 us; the launch traced here: 561 us
  waiting for transfers between devices  338 us (60%)
  matrix products  85.7 us (15%)
  other arithmetic  73.4 us (13%)
  local copies, waits for them, and re-layouts  28.9 us (5%)
  between operations  14.7 us (3%)
  blocking collectives  10.7 us (2%)
  starting transfers between devices  8.84 us (2%)
    ppermute x4, waiting for transfers between devices, swapped(): return lax.ppermute(block, axis, route)  143 us
    reduce_scatter x1, waiting for transfers between devices, on_device(): lax.psum_scatter(partial_out.astype(jnp.bfloat16), 'tp', scatter_dimensio...  80 us
    all_gather x1, waiting for transfers between devices, on_device(): gathered = lax.all_gather(hidden, 'tp', axis=1, tiled=True)  65.6 us
    psum x1, waiting for transfers between devices, on_device(): lax.psum(jnp.dot(final_in, weight, precision=lax.Precision.HIGHEST).astyp...  48.9 us
    dot_general x8, matrix products, fold_piece(): jnp.einsum('hqk,khd->hqd', exps.astype(jnp.bfloat16), key_piece[1], prefe...  39.4 us
    dot_general x8, matrix products, fold_piece(): jnp.einsum('qhd,khd->hqk', queries, key_piece[0], preferred_element_type=...  31.6 us
    reduce_sum x8, other arithmetic, fold_piece(): row_sum = row_sum * decay + jnp.sum(exps, axis=2)  25.9 us
    select_n x3, other arithmetic, on_device(): jnp.where(lower_half, jnp.concatenate([held_keys, far_keys], axis=1), jnp...  17.7 us
  transfers between devices with their start and end apart: 7, of which 7 were waited for; matrix products, arithmetic and copies ran while one was open for 3% of the time, Pallas kernels for 0%

commit v1 on v0

--- a/solution.py
+++ b/solution.py
@@ -116,7 +116,9 @@
     shard_pos = seq_pos % spread
     tp_pos = lax.axis_index("tp")
     local_width = hidden.shape[1]
-    gathered = lax.all_gather(hidden, "tp", axis=1, tiled=True)
+    plain = jnp.stack([hidden for _ in range(lax.axis_size("tp"))], 0)
+    tmp = lax.all_to_all(plain, "tp", 0, 0)
+    gathered = jnp.concatenate(tmp, 1)
     model_width = gathered.shape[1]
     rows_dev = gathered.shape[0]
     layer_terms = lax.dynamic_index_in_dim(layer_mod, local_seq, 0, keepdims=False)

time: 563 us -> 585 us (1.039)
  local copies, waits for them, and re-layouts: 28.9 us -> 44.3 us
  starting transfers between devices: 8.84 us -> 16.4 us
    all_to_all x0 -> x1, waiting for transfers between devices: none -> 66.8 us  [on_device(): tmp = lax.all_to_all(plain, 'tp', 0, 0)]
    all_gather x1 -> x0, waiting for transfers between devices: 65.6 us -> none  [on_device(): gathered = lax.all_gather(hidden, 'tp', axis=1, tiled=True)]
    reduce_scatter x1, waiting for transfers between devices: 80 us -> 67.9 us  [on_device(): lax.psum_scatter(partial_out.astype(jnp.bfloat16), 'tp', scatter_dimensio...]
    convert_element_type x0 -> x2, local copies, waits for them, and re-layouts: none -> 11.9 us  [on_device(): modulate(gathered.astype(jnp.float32), layer_terms[0], layer_terms[1])]
    ppermute x4, waiting for transfers between devices: 143 us -> 151 us  [swapped(): return lax.ppermute(block, axis, route)]
    all_to_all x0 -> x1, starting transfers between devices: none -> 5.89 us  [on_device(): tmp = lax.all_to_all(plain, 'tp', 0, 0)]
where the time goes in v1:
time: 585 us; the launch traced here: 583 us
  waiting for transfers between devices  334 us (57%)
  matrix products  85.5 us (15%)
  other arithmetic  76.8 us (13%)
  local copies, waits for them, and re-layouts  44.3 us (8%)
  starting transfers between devices  16.4 us (3%)
  between operations  15 us (3%)
  blocking collectives  10.8 us (2%)
    ppermute x4, waiting for transfers between devices, swapped(): return lax.ppermute(block, axis, route)  151 us
    reduce_scatter x1, waiting for transfers between devices, on_device(): lax.psum_scatter(partial_out.astype(jnp.bfloat16), 'tp', scatter_dimensio...  67.9 us
    all_to_all x1, waiting for transfers between devices, on_device(): tmp = lax.all_to_all(plain, 'tp', 0, 0)  66.8 us
    psum x1, waiting for transfers between devices, on_device(): lax.psum(jnp.dot(final_in, weight, precision=lax.Precision.HIGHEST).astyp...  48.9 us
    dot_general x8, matrix products, fold_piece(): jnp.einsum('hqk,khd->hqd', exps.astype(jnp.bfloat16), key_piece[1], prefe...  39.4 us
    dot_general x8, matrix products, fold_piece(): jnp.einsum('qhd,khd->hqk', queries, key_piece[0], preferred_element_type=...  31.6 us
    reduce_sum x8, other arithmetic, fold_piece(): row_sum = row_sum * decay + jnp.sum(exps, axis=2)  25.9 us
    select_n x3, other arithmetic, on_device(): jnp.where(lower_half, jnp.concatenate([held_keys, far_keys], axis=1), jnp...  17.7 us
  transfers between devices with their start and end apart: 7, of which 7 were waited for; matrix products, arithmetic and copies ran while one was open for 3% of the time, Pallas kernels for 0%

profile of v1, /device:TPU:2, one launch (start us, length us, event | category | flops | bytes accessed | tf_op | source)
XLA Modules:
  0.0 583.1 jit_solution(3870859374849827114)
XLA Ops:
  10.6 5.9 %all-to-all-start = ((bf16[4,576,768]{2,1,0:T(8,128)(2,1)}), bf16[4,576,768]{2,1,0:T(8,128)(2,1)}, u32[]{:S(2)}, u32[]{:S(2)}) async-start(bf16[4,576,768]{2,1,0:T(8,128)(2,1)} %stack.10), calls=%async_computation | async-start | bytes 7077888 | tf_op jit(solution)/shard_map/all_to_all | solution.py:120
  17.5 10.3 %copy.32 = bf16[3072,3,384]{0,2,1:T(8,128)(2,1)} copy(bf16[3072,3,384]{2,0,1:T(8,128)(2,1)} %param.20) | data formatting | bytes 14155776 | tf_op args[6]
  28.9 66.8 %all-to-all-done = bf16[4,576,768]{2,1,0:T(8,128)(2,1)} async-done(((bf16[4,576,768]{2,1,0:T(8,128)(2,1)}), bf16[4,576,768]{2,1,0:T(8,128)(2,1)}, u32[]{:S(2)}, u32[]{:S(2)}) %all-to-all-start) | async-done | bytes 3538976 | tf_op jit(solution)/shard_map/all_to_all | solution.py:120
  102.4 4.6 copy.31
  107.0 7.3 %reshape.299 = bf16[576,3072,1,1]{1,0,2,3:T(8,128)(2,1)} reshape(bf16[576,4,768]{2,1,0:T(4,128)(2,1)} %copy.31) | data formatting | bytes 7077888 | tf_op jit(solution)/shard_map/convert_element_type | solution.py:126
  114.3 7.7 %fusion.26 = f32[576,3,3,128]{3,0,2,1:T(8,128)S(1)} fusion(bf16[3,3,128,3072]{3,2,1,0:T(8,128)(2,1)} %bitcast.66, bf16[576,3072,1,1]{1,0,2,3:T(8,128)(2,1)} %reshape.299), kind=kOutput, calls=%fused_computation.39 | convolution fusion | flops 4076863488 | bytes 13271040 | tf_op jit(solution)/shard_map/dot_general | solution.py:132
  147.3 6.2 %collective-permute-start = (bf16[2,576,3,128]{3,1,2,0:T(8,128)(2,1)}, bf16[2,576,3,128]{3,1,2,0:T(8,128)(2,1)}, u32[]{:S(2)}, u32[]{:S(2)}) collective-permute-start(bf16[2,576,3,128]{3,1,2,0:T(8,128)(2,1)} %pad_maximum_fusion), channel_id=1, source_target_pairs={{0,4},{4,0},{8,12},{12,8},{16,20},{20,16},{24,28},{28,24},{32,36},... | collective-permute-start | bytes 2654216 | tf_op jit(solution)/shard_map/ppermute | solution.py:23
  153.6 38.6 %collective-permute-done = bf16[2,576,3,128]{3,1,2,0:T(8,128)(2,1)} collective-permute-done((bf16[2,576,3,128]{3,1,2,0:T(8,128)(2,1)}, bf16[2,576,3,128]{3,1,2,0:T(8,128)(2,1)}, u32[]{:S(2)}, u32[]{:S(2)}) %collective-permute-start) | collective-permute-done | bytes 884768 | tf_op jit(solution)/shard_map/ppermute | solution.py:23
  195.8 38.7 %collective-permute-done.1 = bf16[2,1152,3,128]{3,1,2,0:T(8,128)(2,1)} collective-permute-done((bf16[2,1152,3,128]{3,1,2,0:T(8,128)(2,1)}, bf16[2,1152,3,128]{3,1,2,0:T(8,128)(2,1)}, u32[]{:S(2)}, u32[]{:S(2)}) %collective-permute-start.1) | collective-permute-done | bytes 1769504 | tf_op jit(solution)/shard_map/ppermute | solution.py:23
  234.5 5.3 maximum_select_fusion.1
  246.1 71.4 %collective-permute-done.2 = bf16[2,2304,3,128]{3,1,2,0:T(8,128)(2,1)} collective-permute-done((bf16[2,2304,3,128]{3,1,2,0:T(8,128)(2,1)}, bf16[2,2304,3,128]{3,1,2,0:T(8,128)(2,1)}, u32[]{:S(2)}, u32[]{:S(2)}) %collective-permute-start.2) | collective-permute-done | bytes 3538976 | tf_op jit(solution)/shard_map/ppermute | solution.py:23
  317.5 9.3 %maximum_select_fusion = bf16[2,4608,3,128]{3,1,2,0:T(8,128)(2,1)} fusion(bf16[2,2304,3,128]{3,1,2,0:T(8,128)(2,1)} %collective-permute-done.2, bf16[2,2304,3,128]{3,1,2,0:T(8,128)(2,1)} %maximum_select_fusion.1, pred[]{:T(512)S(6)} %eq.18), kind=kLoop, calls=%fused_computation.35 | loop fusion | flops 31850496 | bytes 14155777 | tf_op jit(solution)/shard_map/jit(_where)/select_n | solution.py:153
  326.8 102.5 %while.21 = (s32[]{:T(128)}, f32[3,576]{1,0:T(4,128)S(1)}, f32[3,576]{1,0:T(4,128)S(1)}, f32[3,576,128]{2,1,0:T(8,128)}, s32[]{:T(128)}, /*index=5*/bf16[2,4608,...) while((s32[]{:T(128)}, f32[3,576]{1,0:T(4,128)S(1)}, ...), condition=%wide.region_7.8_spmd.clone.clone, body=%wide.region_4.7_spmd.clone.clone.sunk | while | flops 521231616 | bytes 15596003 | solution.py:95
  334.7 4.7 fusion.69
  347.3 5.0 fusion.69
  360.1 5.0 fusion.69
  372.9 5.0 fusion.69
  385.8 5.0 fusion.69
  398.6 5.0 fusion.69
  411.5 5.0 fusion.69
  424.3 5.0 fusion.69
  436.7 67.9 %reduce-scatter.2.cloned.1.call-done = bf16[576,768]{1,0:T(8,128)(2,1)} async-done(((bf16[576,3072]{1,0:T(8,128)(2,1)}), bf16[576,768]{1,0:T(8,128)(2,1)}) %reduce-scatter.2.cloned.1.call-update) | async-done | bytes 884752 | tf_op jit(solution)/shard_map/reduce_scatter | solution.py:164
  507.3 10.8 %all-reduce = (f32[512]{0:T(512)S(1)}, f32[512]{0:T(512)S(1)}) all-reduce(f32[512]{0:T(512)S(1)} %get-tuple-element.281, f32[512]{0:T(512)S(1)} %get-tuple-element.280), channel_id=1, replica_groups=mesh['pair'=2,'seq'=32,'tp'=4] {'tp'}, use_global_device_ids=true, to_apply=%region_12.13 | all-reduce | flops 1024 | bytes 8192 | tf_op jit(solution)/shard_map/psum | solution.py:176
  521.8 48.9 %all-reduce.3.cloned.1.call-done = bf16[512,64]{0,1:T(8,128)(2,1)} async-done(((bf16[512,64]{0,1:T(8,128)(2,1)}), bf16[512,64]{0,1:T(8,128)(2,1)}) %all-reduce.3.cloned.1.call-update) | async-done | bytes 65552 | tf_op jit(solution)/shard_map/psum | solution.py:182
  (128 shorter events, 128.7 us)
Async XLA Ops:
  7.2 423.9 %copy-start = (bf16[384,3072]{1,0:T(8,128)(2,1)S(1)}, bf16[384,3072]{1,0:T(8,128)(2,1)}, u32[]{:S(2)}) copy-start(bf16[384,3072]{1,0:T(8,128)(2,1)} %param.23) | copy-start | bytes 7077892
  10.6 85.1 %all-to-all-start = ((bf16[4,576,768]{2,1,0:T(8,128)(2,1)}), bf16[4,576,768]{2,1,0:T(8,128)(2,1)}, u32[]{:S(2)}, u32[]{:S(2)}) async-start(bf16[4,576,768]{2,1,0:T(8,128)(2,1)} %stack.10), calls=%async_computation | async-start | bytes 7077888 | tf_op jit(solution)/shard_map/all_to_all | solution.py:120
  16.5 488.1 %reduce-scatter.2.cloned.1.call-start = ((), (), s32[]{:S(2)}) async-start(), calls=%async_computation.2 | async-start | bytes 4423680 | tf_op jit(solution)/shard_map/reduce_scatter | solution.py:164
  17.4 10.3 %copy-start.7 = (f32[128]{0:T(128)S(1)}, f32[128]{0:T(128)}, u32[]{:S(2)}) copy-start(f32[128]{0:T(128)} %param.22) | copy-start | bytes 1540
  17.4 10.4 %copy-start.8 = (f32[128]{0:T(128)S(1)}, f32[128]{0:T(128)}, u32[]{:S(2)}) copy-start(f32[128]{0:T(128)} %param.21) | copy-start | bytes 1540
  17.5 10.6 %copy-start.6 = (s32[3,576]{1,0:T(4,128)S(1)}, s32[3,576]{1,0:T(4,128)}, u32[]{:S(2)}) copy-start(s32[3,576]{1,0:T(4,128)} %param.15) | copy-start | bytes 20740
  147.3 44.8 %collective-permute-start = (bf16[2,576,3,128]{3,1,2,0:T(8,128)(2,1)}, bf16[2,576,3,128]{3,1,2,0:T(8,128)(2,1)}, u32[]{:S(2)}, u32[]{:S(2)}) collective-permute-start(bf16[2,576,3,128]{3,1,2,0:T(8,128)(2,1)} %pad_maximum_fusion), channel_id=1, source_target_pairs={{0,4},{4,0},{8,12},{12,8},{16,20},{20,16},{24,28},{28,24},{32,36},... | collective-permute-start | bytes 2654216 | tf_op jit(solution)/shard_map/ppermute | solution.py:23
  195.3 39.2 %collective-permute-start.1 = (bf16[2,1152,3,128]{3,1,2,0:T(8,128)(2,1)}, bf16[2,1152,3,128]{3,1,2,0:T(8,128)(2,1)}, u32[]{:S(2)}, u32[]{:S(2)}) collective-permute-start(bf16[2,1152,3,128]{3,1,2,0:T(8,128)(2,1)} %maximum_select_fusion.2), channel_id=1, source_target_pairs={{0,8},{8,0},{4,12},{12,4},{16,24},{24,16},{20,28},{28,20},{32,40},... | collective-permute-start | bytes 5308424 | tf_op jit(solution)/shard_map/ppermute | solution.py:23
  195.8 46.1 %copy-start.10 = (s32[4]{0:T(128)S(1)}, s32[4]{0:T(128)}, u32[]{:S(2)}) copy-start(s32[4]{0:T(128)} %param.16) | copy-start | bytes 52
  195.8 46.7 %copy-start.3 = (bf16[576,3,64,1]{0,3,2,1:T(2,128)(2,1)S(1)}, bf16[576,3,64,1]{0,3,2,1:T(2,128)(2,1)}, u32[]{:S(2)}) copy-start(bf16[576,3,64,1]{0,3,2,1:T(2,128)(2,1)} %get-tuple-element.311) | copy-start | bytes 663556
  195.8 46.7 %copy-start.4 = (bf16[576,3,64,1]{0,3,2,1:T(2,128)(2,1)S(1)}, bf16[576,3,64,1]{0,3,2,1:T(2,128)(2,1)}, u32[]{:S(2)}) copy-start(bf16[576,3,64,1]{0,3,2,1:T(2,128)(2,1)} %get-tuple-element.312) | copy-start | bytes 663556
  239.7 77.7 %collective-permute-start.2 = (bf16[2,2304,3,128]{3,1,2,0:T(8,128)(2,1)}, bf16[2,2304,3,128]{3,1,2,0:T(8,128)(2,1)}, u32[]{:S(2)}, u32[]{:S(2)}) collective-permute-start(bf16[2,2304,3,128]{3,1,2,0:T(8,128)(2,1)} %maximum_select_fusion.1), channel_id=1, source_target_pairs={{0,16},{16,0},{4,20},{20,4},{8,24},{24,8},{12,28},{28,12},{32,48},... | collective-permute-start | bytes 10616840 | tf_op jit(solution)/shard_map/ppermute | solution.py:23
  434.8 69.8 %copy-start.1 = (bf16[576,768]{1,0:T(8,128)(2,1)S(1)}, bf16[576,768]{1,0:T(8,128)(2,1)}, u32[]{:S(2)}) copy-start(bf16[576,768]{1,0:T(8,128)(2,1)} %param.14) | copy-start | bytes 2654212
  434.8 83.2 %copy-start.9 = (bf16[768,64]{0,1:T(8,128)(2,1)S(1)}, bf16[768,64]{0,1:T(8,128)(2,1)}, u32[]{:S(2)}) copy-start(bf16[768,64]{0,1:T(8,128)(2,1)} %param.24) | copy-start | bytes 294916
  434.8 140.8 %copy-start.5 = (f32[256,64]{0,1:T(8,128)S(1)}, f32[256,64]{0,1:T(8,128)}, u32[]{:S(2)}) copy-start(f32[256,64]{0,1:T(8,128)} %param.25) | copy-start | bytes 196612
  434.9 135.9 %all-reduce.3.cloned.1.call-start = ((), (), s32[]{:S(2)}) async-start(), calls=%async_computation.3 | async-start | bytes 131072 | tf_op jit(solution)/shard_map/psum | solution.py:182
  506.0 0.9 copy-start.2
  571.6 4.0 collective-permute-start.3
Sparse Core Ops, SparseCore 0:
  435.0 69.5 reduce-scatter.1
  521.2 49.4 all-reduce.2
